TPU v7x, 256 devices: a whole 4x4x8 slice. The times are simulated.
256 devices in a mesh: tile: 64 (over x, z_lo, y), chan: 4 (over z_hi, core).
Axes of the slice: x: 4, y: 4, z: 8 (z_hi: 2, z_lo: 4; z = z_hi * 4 + z_lo), core: 2. Of those that a mesh axis runs over, the one named last changes fastest.
Arguments:
- latlon: bfloat16 [1, 16384, 8, 512], P(None, 'tile', None, 'chan'), may hold values from -6 to 6
- remap_weights: bfloat16 [64, 1156, 2048], P('tile'), may hold values from -0.1875 to 0.1875
- term_source: int32 [64, 256], replicated, may hold values from 0 to 63, as said below
- term_block: int32 [64, 256], replicated, may hold values from 0 to 255
- term_count: int32 [64], replicated, may hold values from 0 to 256, as said below
- rotation: int32 [64], P('tile'), may hold values from 0 to 3
- depthwise: bfloat16 [3, 3, 512], P(None, None, 'chan'), may hold values from -2 to 2
- pointwise: bfloat16 [512, 512], replicated, may hold values from -0.25 to 0.25
- cotangent: bfloat16 [1, 65536, 512], P(None, 'tile', 'chan'), may hold values from -6 to 6
Outputs:
- coupled: bfloat16 [1, 65536, 512], P(None, 'tile', 'chan')
- grad_latlon: bfloat16 [1, 16384, 8, 512], P(None, 'tile', None, 'chan')
- grad_depthwise: float32 [3, 3, 512], P(None, None, 'chan')
- grad_pointwise: float32 [512, 512], P('chan')
Inputs may be any that keep to these rules, and one draw needn't show every extreme that they name: `term_source`: the first term_count[d] entries of row d name the source tile of each term and the rest are 0. Among the used entries of a row no source tile appears more than 6 times, and some row names a tile exactly 6 times. `term_count`: some face tile uses all 256 terms.
All inputs are finite; a program needn't handle non-finite values.
Results may differ from a plain program's by a relative error of at most 0.0059.
Values may be sent and summed in bfloat16 or wider, within the bound.
No kernel may reach another device: no remote copies, remote signals or barrier semaphores. Data moves between devices by JAX's collectives and lax.ppermute only.
A program may use at most 64 MiB of HBM per device.

v0:
```python
import math

import jax
import jax.numpy as jnp
from jax import lax
from jax.sharding import PartitionSpec as P

TILE_EDGE = 32


def turn_kernel(kernel, turn, direction):
    turned = jnp.zeros_like(kernel)
    for quarter in range(4):
        turned = turned + jnp.where(
            turn == quarter, jnp.rot90(kernel, direction * quarter, axes=(0, 1)), 0.0
        )
    return turned


def stencil_apply(field, kernel):
    shape_out = (field.shape[0], TILE_EDGE, TILE_EDGE, field.shape[3])
    hidden = jnp.zeros(shape_out, jnp.float32)
    for row_off in range(3):
        for col_off in range(3):
            window = field[
                :, row_off : row_off + TILE_EDGE, col_off : col_off + TILE_EDGE, :
            ].astype(jnp.float32)
            hidden = hidden + kernel[row_off, col_off] * window
    return hidden


def stencil_grads(field, kernel, grad_hidden):
    tap_rows = []
    grad_field = jnp.zeros(field.shape, jnp.float32)
    for row_off in range(3):
        tap_cols = []
        for col_off in range(3):
            window = field[
                :, row_off : row_off + TILE_EDGE, col_off : col_off + TILE_EDGE, :
            ].astype(jnp.float32)
            tap_cols.append(jnp.sum(window * grad_hidden, axis=(0, 1, 2)))
            spread = kernel[row_off, col_off] * grad_hidden
            grad_field = grad_field + jnp.pad(
                spread, ((0, 0), (row_off, 2 - row_off), (col_off, 2 - col_off), (0, 0))
            )
        tap_rows.append(jnp.stack(tap_cols))
    return (jnp.stack(tap_rows), grad_field)


def body(
    latlon,
    remap_weights,
    term_source,
    term_block,
    term_count,
    rotation,
    depthwise,
    pointwise,
    cotangent,
):
    tile_now = lax.axis_index("tile")
    tile_total = lax.axis_size("tile")
    chan_now = lax.axis_index("chan")
    batch_rows, block_total, seg_len, chan_local = latlon.shape
    terms_max = term_source.shape[1]
    capacity = 3 * terms_max // (2 * tile_total)
    ext_edge = TILE_EDGE + 2
    tile_cells = TILE_EDGE * TILE_EDGE
    flat_rows = batch_rows * tile_cells
    positions = jnp.arange(terms_max, dtype=jnp.int32)
    in_use = positions[None, :] < term_count[:, None]
    mine = in_use & (term_source == tile_now)
    send_rank = jnp.cumsum(mine.astype(jnp.int32), axis=1) - 1
    slot_ids = jnp.arange(capacity, dtype=jnp.int32)
    slot_hits = mine[:, :, None] & (send_rank[:, :, None] == slot_ids[None, None, :])
    slot_filled = jnp.any(slot_hits, axis=1).reshape(-1)
    slot_block = jnp.sum(jnp.where(slot_hits, term_block[:, :, None], 0), axis=1).reshape(-1)
    outgoing = jnp.take(latlon, slot_block, axis=1)
    outgoing = jnp.where(slot_filled[None, :, None, None], outgoing, jnp.zeros((), latlon.dtype))
    own_source = lax.dynamic_index_in_dim(term_source, tile_now, 0, keepdims=False)
    own_count = lax.dynamic_index_in_dim(term_count, tile_now, 0, keepdims=False)
    own_use = positions < own_count
    same_source = (
        (own_source[None, :] == own_source[:, None])
        & own_use[None, :]
        & (positions[None, :] <= positions[:, None])
    )
    own_rank = jnp.sum(same_source.astype(jnp.int32), axis=1) - 1
    recv_slot = jnp.where(own_use, own_source * capacity + own_rank, 0)
    return_slot = jnp.where(own_use, own_source * capacity + own_rank, tile_total * capacity)
    weights = remap_weights[0]
    ext_cells = weights.shape[0]
    term_pts = weights.shape[1]
    arrived = lax.all_to_all(outgoing, "tile", split_axis=1, concat_axis=1, tiled=True)
    picked = jnp.take(arrived, recv_slot, axis=1)
    picked = jnp.where(own_use[None, :, None, None], picked, jnp.zeros((), arrived.dtype))
    picked = picked.reshape(picked.shape[0], term_pts, chan_local)
    mapped = jnp.einsum("pk,bkc->bpc", weights, picked, preferred_element_type=jnp.float32)
    remapped = mapped.astype(jnp.bfloat16)
    field = remapped.reshape(batch_rows, ext_edge, ext_edge, chan_local)
    turn = rotation[0]
    kernel = turn_kernel(depthwise.astype(jnp.float32), turn, 1)
    hidden = stencil_apply(field, kernel)
    active = jax.nn.silu(hidden).astype(jnp.bfloat16).reshape(flat_rows, chan_local)
    own_rows = lax.dynamic_slice_in_dim(pointwise, chan_now * chan_local, chan_local, 0)
    partial_mix = jnp.dot(active, own_rows, preferred_element_type=jnp.float32)
    mixed = lax.psum_scatter(partial_mix, "chan", scatter_dimension=1, tiled=True)
    coupled = mixed.astype(jnp.bfloat16).reshape(batch_rows, tile_cells, chan_local)
    upstream = cotangent.reshape(flat_rows, chan_local)
    piece = lax.all_gather(upstream, "chan", axis=1, tiled=True)
    grad_active = lax.dot_general(
        piece, own_rows, (((1,), (1,)), ((), ())), preferred_element_type=jnp.float32
    )
    block_grad = lax.dot_general(
        active, piece, (((0,), (0,)), ((), ())), preferred_element_type=jnp.float32
    )
    grad_mix = block_grad
    grad_active, grad_mix = (grad_active, grad_mix)
    sigma = jax.nn.sigmoid(hidden)
    grad_hidden = grad_active.reshape(hidden.shape) * sigma * (1.0 + hidden * (1.0 - sigma))
    grad_turned, grad_field = stencil_grads(field, kernel, grad_hidden)
    grad_field = grad_field.astype(jnp.bfloat16).reshape(batch_rows, ext_cells, chan_local)
    grad_terms = jnp.einsum("pk,bpc->bkc", weights, grad_field, preferred_element_type=jnp.float32)
    grad_terms = grad_terms.reshape(batch_rows, terms_max, seg_len, chan_local)
    grad_terms = jnp.where(own_use[None, :, None, None], grad_terms, 0.0).astype(jnp.bfloat16)
    returning = jnp.zeros((batch_rows, tile_total * capacity, seg_len, chan_local), jnp.bfloat16)
    returning = returning.at[:, return_slot].set(grad_terms, mode="drop")
    landing = jnp.where(slot_filled, slot_block, block_total)
    arrived = lax.all_to_all(returning, "tile", split_axis=1, concat_axis=1, tiled=True)
    summed = jnp.zeros((arrived.shape[0], block_total, seg_len, chan_local), jnp.float32)
    summed = summed.at[:, landing].add(arrived.astype(jnp.float32), mode="drop")
    grad_latlon = summed.astype(jnp.bfloat16)
    grad_kernel = turn_kernel(grad_turned, turn, -1)
    kernel_sum, mix_sum = lax.psum((grad_kernel, grad_mix), "tile")
    factor = 1.0 / math.sqrt(batch_rows * tile_cells * tile_total)
    return (coupled, grad_latlon, kernel_sum * factor, mix_sum * factor)


def solution(mesh):
    return jax.shard_map(
        body,
        mesh=mesh,
        in_specs=(
            P(None, "tile", None, "chan"),
            P("tile", None, None),
            P(),
            P(),
            P(),
            P("tile"),
            P(None, None, "chan"),
            P(),
            P(None, "tile", "chan"),
        ),
        out_specs=(
            P(None, "tile", "chan"),
            P(None, "tile", None, "chan"),
            P(None, None, "chan"),
            P("chan", None),
        ),
        check_vma=False,
    )
```

profile of v0, /device:TPU:8, one launch (start us, length us, event | category | flops | bytes accessed | tf_op | source)
XLA Modules:
  0.0 796.1 jit_solution(1122803104299153923)
XLA Ops:
  7.2 1.0 convert_bitcast_fusion.2
  9.3 1.0 select_reduce_fusion
  11.2 1.7 gather_fusion
  13.0 3.1 fusion.17
  16.1 12.0 %all-to-all-start = ((bf16[1,384,8,128]{3,2,0,1:T(8,128)(2,1)}), bf16[1,384,8,128]{3,2,0,1:T(8,128)(2,1)S(1)}, u32[]{:S(2)}, u32[]{:S(2)}) async-start(bf16[1,384,8,128]{3,2,0,1:T(8,128)(2,1)} %fusion.17), calls=%async_computation | async-start | bytes 1572864 | tf_op jit(solution)/shard_map/all_to_all | solution.py:94
  28.2 0.7 all-gather.3.cloned.1.call-update
  29.5 0.7 constant_dynamic-slice_fusion
  30.2 0.6 iota_compare_fusion.3
  31.0 1.4 compare_select_fusion.2
  33.1 0.7 compare_and_fusion.1
  33.9 17.1 %all-to-all-done = bf16[1,384,8,128]{3,2,0,1:T(8,128)(2,1)S(1)} async-done(((bf16[1,384,8,128]{3,2,0,1:T(8,128)(2,1)}), bf16[1,384,8,128]{3,2,0,1:T(8,128)(2,1)S(1)}, u32[]{:S(2)}, u32[]{:S(2)}) %all-to-all-start) | async-done | bytes 786464 | tf_op jit(solution)/shard_map/all_to_all | solution.py:94
  50.9 0.8 gather_fusion.1
  51.7 3.9 fusion.10
  55.8 2.6 all-gather.3.cloned.1.call-done
  58.4 1.8 convolution_bitcast_fusion
  60.3 0.9 fusion.26
  61.3 1.8 broadcast_multiply_fusion.8
  63.1 1.0 fusion.14
  64.2 2.7 fusion.47
  66.9 2.8 add_convert_fusion
  69.6 1.1 reshape.359
  70.7 3.3 fusion.4
  74.6 1.0 broadcast.366
  75.6 23.3 %scatter_fusion = bf16[384,8,128]{2,1,0:T(8,128)(2,1)} fusion(bf16[384,8,128]{2,1,0:T(8,128)(2,1)} %broadcast.366, s32[256]{0:T(256)S(1)} %bitcast.143, bf16[256,8,128]{2,1,0:T(8,128)(2,1)S(1)} %fusion.35), kind=kCustom, calls=%fused_computation.2 | custom fusion | bytes 1573888 | tf_op jit(solution)/shard_map/scatter | solution.py:127
  99.0 13.7 %all-to-all-start.1 = ((bf16[1,384,8,128]{3,2,0,1:T(8,128)(2,1)}), bf16[1,384,8,128]{3,2,0,1:T(8,128)(2,1)S(1)}, u32[]{:S(2)}, u32[]{:S(2)}) async-start(bf16[1,384,8,128]{3,2,0,1:T(8,128)(2,1)} %bitcast.38), calls=%async_computation.2 | async-start | bytes 1572864 | tf_op jit(solution)/shard_map/all_to_all | solution.py:129
  112.9 194.0 %psum.14 = f32[3,3,128]{2,0,1:T(4,128)S(1)} all-reduce(f32[3,3,128]{2,0,1:T(4,128)S(1)} %bitcast_add_fusion), channel_id=1, replica_groups=mesh['tile'=64,'chan'=4] {'tile'}, use_global_device_ids=true, to_apply=%region_17.18 | all-reduce | flops 1152 | bytes 9216 | tf_op jit(solution)/shard_map/psum | solution.py:134
  307.4 422.2 %all-reduce.11.cloned.1.call-done = f32[128,512]{1,0:T(8,128)} async-done(((f32[128,512]{1,0:T(8,128)}), f32[128,512]{1,0:T(8,128)}) %all-reduce.11.cloned.1.call-update) | async-done | bytes 262160 | tf_op jit(solution)/shard_map/psum | solution.py:134
  729.7 1.7 broadcast_multiply_fusion.9
  731.5 14.8 %scatter_fusion.1 = f32[256,8,128]{2,1,0:T(8,128)S(1)} fusion(f32[256,8,128]{2,1,0:T(8,128)S(1)} %broadcast.367, s32[384]{0:T(512)S(1)} %get-tuple-element.29, f32[384,8,128]{2,1,0:T(8,128)S(1)} %bitcast_convert_fusion), kind=kCustom, calls=%fused_computation.3 | custom fusion | flops 393216 | bytes 4720128 | tf_op jit(solution)/shard_map/scatter-add | solution.py:131
  746.3 0.8 convert_bitcast_fusion
  747.2 40.6 %reduce-scatter.2.cloned.1.call-done = f32[1024,128]{1,0:T(8,128)} async-done(((f32[1024,512]{1,0:T(8,128)}), f32[1024,128]{1,0:T(8,128)}) %reduce-scatter.2.cloned.1.call-update) | async-done | bytes 524304 | tf_op jit(solution)/shard_map/reduce_scatter | solution.py:107
  787.8 1.8 convert_bitcast_fusion.1
  (55 shorter events, 4.8 us)
Async XLA Ops:
  7.2 4.1 copy-start
  7.2 21.7 %copy-start.3 = (s32[64]{0:T(128)S(1)}, s32[64]{0:T(128)}, u32[]{:S(2)}) copy-start(s32[64]{0:T(128)} %param.13) | copy-start | bytes 772
  7.2 25.2 %copy-start.2 = (bf16[3,3,128]{2,1,0:T(4,128)(2,1)S(1)}, bf16[3,3,128]{2,1,0:T(4,128)(2,1)}, u32[]{:S(2)}) copy-start(bf16[3,3,128]{2,1,0:T(4,128)(2,1)} %param.15) | copy-start | bytes 6916
  16.1 34.8 %all-to-all-start = ((bf16[1,384,8,128]{3,2,0,1:T(8,128)(2,1)}), bf16[1,384,8,128]{3,2,0,1:T(8,128)(2,1)S(1)}, u32[]{:S(2)}, u32[]{:S(2)}) async-start(bf16[1,384,8,128]{3,2,0,1:T(8,128)(2,1)} %fusion.17), calls=%async_computation | async-start | bytes 1572864 | tf_op jit(solution)/shard_map/all_to_all | solution.py:94
  28.1 30.3 %all-gather.3.cloned.1.call-start = ((), (), s32[]{:S(2)}) async-start(), calls=%async_computation.5 | async-start | bytes 1310720 | tf_op jit(solution)/shard_map/all_gather | solution.py:110
  28.8 700.8 %all-reduce.11.cloned.1.call-start = ((), (), s32[]{:S(2)}) async-start(), calls=%async_computation.4 | async-start | bytes 524288 | tf_op jit(solution)/shard_map/psum | solution.py:134
  60.3 2.7 copy-start.1
  64.1 723.7 %reduce-scatter.2.cloned.1.call-start = ((), (), s32[]{:S(2)}) async-start(), calls=%async_computation.3 | async-start | bytes 2621440 | tf_op jit(solution)/shard_map/reduce_scatter | solution.py:107
  99.0 632.4 %all-to-all-start.1 = ((bf16[1,384,8,128]{3,2,0,1:T(8,128)(2,1)}), bf16[1,384,8,128]{3,2,0,1:T(8,128)(2,1)S(1)}, u32[]{:S(2)}, u32[]{:S(2)}) async-start(bf16[1,384,8,128]{3,2,0,1:T(8,128)(2,1)} %bitcast.38), calls=%async_computation.2 | async-start | bytes 1572864 | tf_op jit(solution)/shard_map/all_to_all | solution.py:129
Sparse Core Ops, SparseCore 0:
  30.7 27.5 all-gather.2
  64.2 665.3 all-reduce.10
  732.5 55.3 reduce-scatter.1
where the time goes:
time: 798 us; the launch traced here: 796 us
  waiting for transfers between devices  483 us (61%)
  blocking collectives  194 us (24%)
  other arithmetic  34 us (4%)
  local copies, waits for them, and re-layouts  31.6 us (4%)
  starting transfers between devices  25.9 us (3%)
  between operations  14.7 us (2%)
  matrix products  12.7 us (2%)
    psum x1, waiting for transfers between devices, body(): kernel_sum, mix_sum = lax.psum((grad_kernel, grad_mix), 'tile')  422 us
    psum x1, blocking collectives, body(): kernel_sum, mix_sum = lax.psum((grad_kernel, grad_mix), 'tile')  194 us
    reduce_scatter x1, waiting for transfers between devices, body(): lax.psum_scatter(partial_mix, 'chan', scatter_dimension=1, tiled=True)  40.6 us
    scatter x1, local copies, waits for them, and re-layouts, body(): returning = returning.at[:, return_slot].set(grad_terms, mode='drop')  23.3 us
    all_to_all x1, waiting for transfers between devices, body(): lax.all_to_all(outgoing, 'tile', split_axis=1, concat_axis=1, tiled=True)  17.1 us
  transfers between devices with their start and end apart: 5, of which 4 were waited for; matrix products, arithmetic and copies ran while one was open for 8% of the time, Pallas kernels for 0%

commit v1 on v0

--- a/solution.py
+++ b/solution.py
@@ -3,9 +3,11 @@
 import jax
 import jax.numpy as jnp
 from jax import lax
-from jax.sharding import PartitionSpec as P
+from jax.sharding import Mesh, PartitionSpec as P
 
 TILE_EDGE = 32
+TILE = ("x", "zl", "y")
+CHAN = ("zh", "core")
 
 
 def turn_kernel(kernel, turn, direction):
@@ -58,9 +60,9 @@
     pointwise,
     cotangent,
 ):
-    tile_now = lax.axis_index("tile")
-    tile_total = lax.axis_size("tile")
-    chan_now = lax.axis_index("chan")
+    tile_now = lax.axis_index(TILE)
+    tile_total = term_source.shape[0]
+    chan_now = lax.axis_index(CHAN)
     batch_rows, block_total, seg_len, chan_local = latlon.shape
     terms_max = term_source.shape[1]
     capacity = 3 * terms_max // (2 * tile_total)
@@ -91,7 +93,7 @@
     weights = remap_weights[0]
     ext_cells = weights.shape[0]
     term_pts = weights.shape[1]
-    arrived = lax.all_to_all(outgoing, "tile", split_axis=1, concat_axis=1, tiled=True)
+    arrived = lax.all_to_all(outgoing, TILE, split_axis=1, concat_axis=1, tiled=True)
     picked = jnp.take(arrived, recv_slot, axis=1)
     picked = jnp.where(own_use[None, :, None, None], picked, jnp.zeros((), arrived.dtype))
     picked = picked.reshape(picked.shape[0], term_pts, chan_local)
@@ -103,11 +105,12 @@
     hidden = stencil_apply(field, kernel)
     active = jax.nn.silu(hidden).astype(jnp.bfloat16).reshape(flat_rows, chan_local)
     own_rows = lax.dynamic_slice_in_dim(pointwise, chan_now * chan_local, chan_local, 0)
-    partial_mix = jnp.dot(active, own_rows, preferred_element_type=jnp.float32)
-    mixed = lax.psum_scatter(partial_mix, "chan", scatter_dimension=1, tiled=True)
+    own_cols = lax.dynamic_slice_in_dim(pointwise, chan_now * chan_local, chan_local, 1)
+    active_all = lax.all_gather(active, CHAN, axis=1, tiled=True)
+    mixed = jnp.dot(active_all, own_cols, preferred_element_type=jnp.float32)
     coupled = mixed.astype(jnp.bfloat16).reshape(batch_rows, tile_cells, chan_local)
     upstream = cotangent.reshape(flat_rows, chan_local)
-    piece = lax.all_gather(upstream, "chan", axis=1, tiled=True)
+    piece = lax.all_gather(upstream, CHAN, axis=1, tiled=True)
     grad_active = lax.dot_general(
         piece, own_rows, (((1,), (1,)), ((), ())), preferred_element_type=jnp.float32
     )
@@ -126,36 +129,53 @@
     returning = jnp.zeros((batch_rows, tile_total * capacity, seg_len, chan_local), jnp.bfloat16)
     returning = returning.at[:, return_slot].set(grad_terms, mode="drop")
     landing = jnp.where(slot_filled, slot_block, block_total)
-    arrived = lax.all_to_all(returning, "tile", split_axis=1, concat_axis=1, tiled=True)
+    arrived = lax.all_to_all(returning, TILE, split_axis=1, concat_axis=1, tiled=True)
     summed = jnp.zeros((arrived.shape[0], block_total, seg_len, chan_local), jnp.float32)
     summed = summed.at[:, landing].add(arrived.astype(jnp.float32), mode="drop")
     grad_latlon = summed.astype(jnp.bfloat16)
     grad_kernel = turn_kernel(grad_turned, turn, -1)
-    kernel_sum, mix_sum = lax.psum((grad_kernel, grad_mix), "tile")
+    packed = jnp.concatenate([grad_kernel.reshape(-1), grad_mix.reshape(-1)])
+    for axis in TILE:
+        packed = lax.psum(packed, axis)
+    kernel_sum = packed[: grad_kernel.size].reshape(grad_kernel.shape)
+    mix_sum = packed[grad_kernel.size :].reshape(grad_mix.shape)
     factor = 1.0 / math.sqrt(batch_rows * tile_cells * tile_total)
     return (coupled, grad_latlon, kernel_sum * factor, mix_sum * factor)
 
 
+def physical_mesh(mesh):
+    devices = mesh.devices
+    tile_devs = devices[:, 0]
+    x_count = len({d.coords[0] for d in tile_devs})
+    y_count = len({d.coords[1] for d in tile_devs})
+    zl_count = tile_devs.size // (x_count * y_count)
+    zh_count = len({d.coords[2] for d in devices[0, :]})
+    core_count = devices.shape[1] // zh_count
+    shaped = devices.reshape(x_count, zl_count, y_count, zh_count, core_count)
+    return Mesh(shaped, TILE + CHAN)
+
+
 def solution(mesh):
+    mesh = physical_mesh(mesh)
     return jax.shard_map(
         body,
         mesh=mesh,
         in_specs=(
-            P(None, "tile", None, "chan"),
-            P("tile", None, None),
+            P(None, TILE, None, CHAN),
+            P(TILE, None, None),
             P(),
             P(),
             P(),
-            P("tile"),
-            P(None, None, "chan"),
+            P(TILE),
+            P(None, None, CHAN),
             P(),
-            P(None, "tile", "chan"),
+            P(None, TILE, CHAN),
         ),
         out_specs=(
-            P(None, "tile", "chan"),
-            P(None, "tile", None, "chan"),
-            P(None, None, "chan"),
-            P("chan", None),
+            P(None, TILE, CHAN),
+            P(None, TILE, None, CHAN),
+            P(None, None, CHAN),
+            P(CHAN, None),
         ),
         check_vma=False,
     )

time: 798 us -> 261 us (0.33)
  waiting for transfers between devices: 483 us -> 149 us
  blocking collectives: 194 us -> 0 us
    psum x1 -> x3, waiting for transfers between devices: 422 us -> 112 us  [body(): packed = lax.psum(packed, axis)]
    psum x1 -> x0, blocking collectives: 194 us -> none  [body(): kernel_sum, mix_sum = lax.psum((grad_kernel, grad_mix), 'tile')]
    reduce_scatter x1 -> x0, waiting for transfers between devices: 40.6 us -> none  [body(): lax.psum_scatter(partial_mix, 'chan', scatter_dimension=1, tiled=True)]
    all_gather x1 -> x2, waiting for transfers between devices: 2.6 us -> 11.4 us  [the longest x1 8.79 us: body(): active_all = lax.all_gather(active, CHAN, axis=1, tiled=True)]
  transfers between devices with their start and end apart: 5 -> 7, of which waited for: 4 -> 7; matrix products, arithmetic and copies ran while one was open for 8% -> 23% of each run, Pallas kernels for 0% -> 0%
where the time goes in v1:
time: 261 us; the launch traced here: 258 us
  waiting for transfers between devices  149 us (57%)
  local copies, waits for them, and re-layouts  32.5 us (12%)
  other arithmetic  29.9 us (11%)
  starting transfers between devices  20.5 us (8%)
  between operations  14.8 us (6%)
  matrix products  11.8 us (5%)
    psum x3, waiting for transfers between devices, body(): packed = lax.psum(packed, axis)  112 us
    scatter x1, local copies, waits for them, and re-layouts, body(): returning = returning.at[:, return_slot].set(grad_terms, mode='drop')  24.3 us
    all_to_all x1, waiting for transfers between devices, body(): lax.all_to_all(outgoing, TILE, split_axis=1, concat_axis=1, tiled=True)  17.1 us
    scatter-add x1, other arithmetic, body(): summed = summed.at[:, landing].add(arrived.astype(jnp.float32), mode='drop')  14.8 us
    all_to_all x1, starting transfers between devices, body(): lax.all_to_all(outgoing, TILE, split_axis=1, concat_axis=1, tiled=True)  12 us
    all_gather x1, waiting for transfers between devices, body(): active_all = lax.all_gather(active, CHAN, axis=1, tiled=True)  8.79 us
    all_to_all x1, starting transfers between devices, body(): lax.all_to_all(returning, TILE, split_axis=1, concat_axis=1, tiled=True)  8.32 us
    all_to_all x1, waiting for transfers between devices, body(): lax.all_to_all(returning, TILE, split_axis=1, concat_axis=1, tiled=True)  7.15 us
  transfers between devices with their start and end apart: 7, of which 7 were waited for; matrix products, arithmetic and copies ran while one was open for 23% of the time, Pallas kernels for 0%

profile of v1, /device:TPU:8, one launch (start us, length us, event | category | flops | bytes accessed | tf_op | source)
XLA Modules:
  0.0 258.4 jit_solution(9863386729955952436)
XLA Ops:
  7.2 1.0 convert_bitcast_fusion.1
  9.3 1.0 select_reduce_fusion
  11.2 1.7 gather_fusion
  13.0 3.1 %fusion.17 = bf16[1,384,8,128]{3,2,0,1:T(8,128)(2,1)} fusion(bf16[384,8,128]{2,1,0:T(8,128)(2,1)S(1)} %gather_fusion, pred[384]{0:T(512)(128)(4,1)S(1)} %compare_and_fusion, pred[384]{0:T(512)(128)(4,1)S(1)} %broadcast_in_dim.109), kind=kLoop, calls=%fused_computation.21 | loop fusion | flops 786432 | bytes 1573632 | tf_op jit(solution)/shard_map/jit(_where)/select_n | solution.py:81
  16.1 12.0 %all-to-all-start = ((bf16[1,384,8,128]{3,2,0,1:T(8,128)(2,1)}), bf16[1,384,8,128]{3,2,0,1:T(8,128)(2,1)S(1)}, u32[]{:S(2)}, u32[]{:S(2)}) async-start(bf16[1,384,8,128]{3,2,0,1:T(8,128)(2,1)} %fusion.17), calls=%async_computation | async-start | bytes 1572864 | tf_op jit(solution)/shard_map/all_to_all | solution.py:96
  28.2 0.7 all-gather.6.cloned.1.call-update
  29.5 0.7 constant_dynamic-slice_fusion
  31.0 1.4 compare_select_fusion.2
  33.1 0.7 compare_and_fusion.1
  33.9 17.1 %all-to-all-done = bf16[1,384,8,128]{3,2,0,1:T(8,128)(2,1)S(1)} async-done(((bf16[1,384,8,128]{3,2,0,1:T(8,128)(2,1)}), bf16[1,384,8,128]{3,2,0,1:T(8,128)(2,1)S(1)}, u32[]{:S(2)}, u32[]{:S(2)}) %all-to-all-start) | async-done | bytes 786464 | tf_op jit(solution)/shard_map/all_to_all | solution.py:96
  50.9 0.8 gather_fusion.1
  51.7 3.9 %fusion.10 = bf16[1,1156,128]{2,1,0:T(8,128)(2,1)S(1)} fusion(bf16[1,1156,2048]{2,1,0:T(8,128)(2,1)} %param.10, bf16[256,8,128]{2,1,0:T(8,128)(2,1)S(1)} %gather_fusion.1, pred[256]{0:T(512)(128)(4,1)S(1)} %compare_and_fusion.1, pred[256]{0:T(512)(128)(4,1)S(1)} %iota_compare_fusion.3), kind=kOutput, calls=%fused_computation.10 | convolution fusion | flops 606749184 | bytes 5555712 | tf_op jit(solution)/shard_map/pk,bkc->bpc/dot_general | solution.py:100
  55.8 2.6 %all-gather.6.cloned.1.call-done = bf16[1,1024,512]{2,1,0:T(8,128)(2,1)} async-done(((bf16[1,1024,128]{2,1,0:T(8,128)(2,1)}), bf16[1,1024,512]{2,1,0:T(8,128)(2,1)}) %all-gather.6.cloned.1.call-update) | async-done | bytes 1048592 | tf_op jit(solution)/shard_map/all_gather | solution.py:113
  58.4 1.8 convolution_bitcast_fusion
  60.4 0.9 fusion.26
  62.1 0.7 pad_maximum_fusion
  62.9 51.0 %all-reduce.13.cloned.1.call-done = f32[66688]{0:T(1024)} async-done(((f32[66688]{0:T(1024)}), f32[66688]{0:T(1024)}) %all-reduce.13.cloned.1.call-update) | async-done | bytes 266768 | tf_op jit(solution)/shard_map/psum | solution.py:139
  114.6 0.7 add_convert_fusion
  115.4 51.1 %all-reduce.15.cloned.1.call-done = f32[66688]{0:T(1024)} async-done(((f32[66688]{0:T(1024)}), f32[66688]{0:T(1024)}) %all-reduce.15.cloned.1.call-update) | async-done | bytes 266768 | tf_op jit(solution)/shard_map/psum | solution.py:139
  166.5 3.3 %fusion.4 = bf16[1,2048,128]{1,2,0:T(8,128)(2,1)S(1)} fusion(bf16[1156,128]{1,0:T(8,128)(2,1)S(1)} %reshape.371, bf16[1,1156,2048]{2,1,0:T(8,128)(2,1)} %param.10), kind=kOutput, calls=%fused_computation.8 | convolution fusion | flops 606076928 | bytes 5555200 | tf_op jit(solution)/shard_map/pk,bpc->bkc/dot_general | solution.py:126
  170.4 1.0 broadcast.370
  171.5 24.3 %scatter_fusion = bf16[384,8,128]{2,1,0:T(8,128)(2,1)} fusion(bf16[384,8,128]{2,1,0:T(8,128)(2,1)} %broadcast.370, s32[256]{0:T(256)S(1)} %bitcast.147, bf16[256,8,128]{2,1,0:T(8,128)(2,1)S(1)} %fusion.35), kind=kCustom, calls=%fused_computation.2 | custom fusion | bytes 1573888 | tf_op jit(solution)/shard_map/scatter | solution.py:130
  195.8 8.3 %all-to-all-start.1 = ((bf16[1,384,8,128]{3,2,0,1:T(8,128)(2,1)}), bf16[1,384,8,128]{3,2,0,1:T(8,128)(2,1)S(1)}, u32[]{:S(2)}, u32[]{:S(2)}) async-start(bf16[1,384,8,128]{3,2,0,1:T(8,128)(2,1)} %bitcast.38), calls=%async_computation.1 | async-start | bytes 1572864 | tf_op jit(solution)/shard_map/all_to_all | solution.py:132
  204.7 10.0 %all-reduce.17.cloned.1.call-done = f32[66688]{0:T(1024)} async-done(((f32[66688]{0:T(1024)}), f32[66688]{0:T(1024)}) %all-reduce.17.cloned.1.call-update) | async-done | bytes 266768 | tf_op jit(solution)/shard_map/psum | solution.py:139
  214.7 1.0 slice_multiply_fusion
  215.7 0.7 mul.298
  216.4 0.7 slice_multiply_fusion.1
  217.7 7.1 %all-to-all-done.1 = bf16[1,384,8,128]{3,2,0,1:T(8,128)(2,1)S(1)} async-done(((bf16[1,384,8,128]{3,2,0,1:T(8,128)(2,1)}), bf16[1,384,8,128]{3,2,0,1:T(8,128)(2,1)S(1)}, u32[]{:S(2)}, u32[]{:S(2)}) %all-to-all-start.1) | async-done | bytes 786464 | tf_op jit(solution)/shard_map/all_to_all | solution.py:132
  225.0 14.8 %scatter_fusion.1 = f32[256,8,128]{2,1,0:T(8,128)S(1)} fusion(f32[256,8,128]{2,1,0:T(8,128)S(1)} %broadcast.371, s32[384]{0:T(512)S(1)} %get-tuple-element.13, f32[384,8,128]{2,1,0:T(8,128)S(1)} %bitcast_convert_fusion), kind=kCustom, calls=%fused_computation.3 | custom fusion | flops 393216 | bytes 4720128 | tf_op jit(solution)/shard_map/scatter-add | solution.py:134
  239.8 0.8 convert_bitcast_fusion
  240.7 8.8 %all-gather.4.cloned.1.call-done = bf16[1024,512]{1,0:T(8,128)(2,1)} async-done(((bf16[1024,128]{1,0:T(8,128)(2,1)}), bf16[1024,512]{1,0:T(8,128)(2,1)}) %all-gather.4.cloned.1.call-update) | async-done | bytes 1048592 | tf_op jit(solution)/shard_map/all_gather | solution.py:109
  249.5 2.4 fusion.13
  (67 shorter events, 7.3 us)
Async XLA Ops:
  7.2 4.1 %copy-start = (bf16[1,256,8,128]{3,2,1,0:T(8,128)(2,1)S(1)}, bf16[1,256,8,128]{3,2,1,0:T(8,128)(2,1)}, u32[]{:S(2)}) copy-start(bf16[1,256,8,128]{3,2,1,0:T(8,128)(2,1)} %param.9) | copy-start | bytes 1572868
  7.2 21.7 %copy-start.4 = (s32[64]{0:T(128)S(1)}, s32[64]{0:T(128)}, u32[]{:S(2)}) copy-start(s32[64]{0:T(128)} %param.13) | copy-start | bytes 772
  7.2 25.2 %copy-start.3 = (bf16[3,3,128]{2,1,0:T(4,128)(2,1)S(1)}, bf16[3,3,128]{2,1,0:T(4,128)(2,1)}, u32[]{:S(2)}) copy-start(bf16[3,3,128]{2,1,0:T(4,128)(2,1)} %param.15) | copy-start | bytes 6916
  16.1 34.8 %all-to-all-start = ((bf16[1,384,8,128]{3,2,0,1:T(8,128)(2,1)}), bf16[1,384,8,128]{3,2,0,1:T(8,128)(2,1)S(1)}, u32[]{:S(2)}, u32[]{:S(2)}) async-start(bf16[1,384,8,128]{3,2,0,1:T(8,128)(2,1)} %fusion.17), calls=%async_computation | async-start | bytes 1572864 | tf_op jit(solution)/shard_map/all_to_all | solution.py:96
  28.1 30.3 %all-gather.6.cloned.1.call-start = ((), (), s32[]{:S(2)}) async-start(), calls=%async_computation.6 | async-start | bytes 1310720 | tf_op jit(solution)/shard_map/all_gather | solution.py:113
  28.8 85.0 %all-reduce.13.cloned.1.call-start = ((), (), s32[]{:S(2)}) async-start(), calls=%async_computation.3 | async-start | bytes 540672 | tf_op jit(solution)/shard_map/psum | solution.py:139
  58.4 3.3 %copy-start.1 = (bf16[1,1024,512]{2,1,0:T(8,128)(2,1)S(1)}, bf16[1,1024,512]{2,1,0:T(8,128)(2,1)}, u32[]{:S(2)}) copy-start(bf16[1,1024,512]{2,1,0:T(8,128)(2,1)} %all-gather.6.cloned.1.call-done) | copy-start | bytes 3145732
  61.7 53.6 %copy-start.2 = (bf16[1,32,32,128]{3,2,1,0:T(8,128)(2,1)}, bf16[1,32,32,128]{3,2,1,0:T(8,128)(2,1)S(1)}, u32[]{:S(2)}) copy-start(bf16[1,32,32,128]{3,2,1,0:T(8,128)(2,1)S(1)} %multiply_convert_fusion) | copy-start | bytes 786436
  62.9 103.6 %all-reduce.15.cloned.1.call-start = ((), (), s32[]{:S(2)}) async-start(), calls=%async_computation.4 | async-start | bytes 540672 | tf_op jit(solution)/shard_map/psum | solution.py:139
  113.9 100.8 %all-reduce.17.cloned.1.call-start = ((), (), s32[]{:S(2)}) async-start(), calls=%async_computation.5 | async-start | bytes 540672 | tf_op jit(solution)/shard_map/psum | solution.py:139
  195.8 29.1 %all-to-all-start.1 = ((bf16[1,384,8,128]{3,2,0,1:T(8,128)(2,1)}), bf16[1,384,8,128]{3,2,0,1:T(8,128)(2,1)S(1)}, u32[]{:S(2)}, u32[]{:S(2)}) async-start(bf16[1,384,8,128]{3,2,0,1:T(8,128)(2,1)} %bitcast.38), calls=%async_computation.1 | async-start | bytes 1572864 | tf_op jit(solution)/shard_map/all_to_all | solution.py:132
  204.1 45.3 %all-gather.4.cloned.1.call-start = ((), (), s32[]{:S(2)}) async-start(), calls=%async_computation.2 | async-start | bytes 1310720 | tf_op jit(solution)/shard_map/all_gather | solution.py:109
Sparse Core Ops, SparseCore 0:
  30.7 27.5 all-gather.5
  63.0 50.8 all-reduce.12
  116.5 49.9 all-reduce.14
  168.7 45.9 all-reduce.16
  216.9 32.5 all-gather.3

commit v2 on v1

--- a/solution.py
+++ b/solution.py
@@ -47,6 +47,17 @@
             )
         tap_rows.append(jnp.stack(tap_cols))
     return (jnp.stack(tap_rows), grad_field)
+
+
+def tile_sum(flat, parts):
+    total = flat.shape[0]
+    width = -(-total // (parts * 128)) * 128
+    rows = jnp.pad(flat, (0, parts * width - total)).reshape(parts, width)
+    pieces = lax.all_to_all(rows, TILE, split_axis=0, concat_axis=0, tiled=True)
+    mine = jnp.sum(pieces, axis=0)
+    spread = jnp.broadcast_to(mine[None, :], (parts, width))
+    whole = lax.all_to_all(spread, TILE, split_axis=0, concat_axis=0, tiled=True)
+    return whole.reshape(-1)[:total]
 
 
 def body(
@@ -126,17 +137,24 @@
     grad_terms = jnp.einsum("pk,bpc->bkc", weights, grad_field, preferred_element_type=jnp.float32)
     grad_terms = grad_terms.reshape(batch_rows, terms_max, seg_len, chan_local)
     grad_terms = jnp.where(own_use[None, :, None, None], grad_terms, 0.0).astype(jnp.bfloat16)
-    returning = jnp.zeros((batch_rows, tile_total * capacity, seg_len, chan_local), jnp.bfloat16)
-    returning = returning.at[:, return_slot].set(grad_terms, mode="drop")
+    slot_all = jnp.arange(tile_total * capacity, dtype=jnp.int32)
+    place = (slot_all[:, None] == return_slot[None, :]).astype(jnp.bfloat16)
+    returning = jnp.einsum(
+        "st,btc->bsc", place, grad_terms.reshape(batch_rows, terms_max, seg_len * chan_local),
+        preferred_element_type=jnp.float32,
+    ).astype(jnp.bfloat16).reshape(batch_rows, tile_total * capacity, seg_len, chan_local)
     landing = jnp.where(slot_filled, slot_block, block_total)
     arrived = lax.all_to_all(returning, TILE, split_axis=1, concat_axis=1, tiled=True)
-    summed = jnp.zeros((arrived.shape[0], block_total, seg_len, chan_local), jnp.float32)
-    summed = summed.at[:, landing].add(arrived.astype(jnp.float32), mode="drop")
-    grad_latlon = summed.astype(jnp.bfloat16)
+    block_ids = jnp.arange(block_total, dtype=jnp.int32)
+    gather_back = (block_ids[:, None] == landing[None, :]).astype(jnp.bfloat16)
+    summed = jnp.einsum(
+        "ks,bsc->bkc", gather_back, arrived.reshape(batch_rows, tile_total * capacity, seg_len * chan_local),
+        preferred_element_type=jnp.float32,
+    )
+    grad_latlon = summed.astype(jnp.bfloat16).reshape(batch_rows, block_total, seg_len, chan_local)
     grad_kernel = turn_kernel(grad_turned, turn, -1)
     packed = jnp.concatenate([grad_kernel.reshape(-1), grad_mix.reshape(-1)])
-    for axis in TILE:
-        packed = lax.psum(packed, axis)
+    packed = tile_sum(packed, tile_total)
     kernel_sum = packed[: grad_kernel.size].reshape(grad_kernel.shape)
     mix_sum = packed[grad_kernel.size :].reshape(grad_mix.shape)
     factor = 1.0 / math.sqrt(batch_rows * tile_cells * tile_total)

time: 261 us -> 158 us (0.61)
  waiting for transfers between devices: 149 us -> 75.7 us
  local copies, waits for them, and re-layouts: 32.5 us -> 10.5 us
  other arithmetic: 29.9 us -> 13.7 us
  starting transfers between devices: 20.5 us -> 29.2 us
    psum x3 -> x0, waiting for transfers between devices: 112 us -> none  [body(): packed = lax.psum(packed, axis)]
    all_to_all x0 -> x2, waiting for transfers between devices: none -> 26.1 us  [the longest x1 16.1 us: tile_sum(): lax.all_to_all(spread, TILE, split_axis=0, concat_axis=0, tiled=True)]
    scatter x1 -> x0, local copies, waits for them, and re-layouts: 24.3 us -> none  [body(): returning = returning.at[:, return_slot].set(grad_terms, mode='drop')]
    scatter-add x1 -> x0, other arithmetic: 14.8 us -> none  [body(): summed = summed.at[:, landing].add(arrived.astype(jnp.float32), mode='drop')]
    all_to_all x1, waiting for transfers between devices: 7.15 us -> 21.6 us  [body(): lax.all_to_all(returning, TILE, split_axis=1, concat_axis=1, tiled=True)]
    all_to_all x0 -> x2, starting transfers between devices: none -> 11.6 us  [the longest x1 6.06 us: tile_sum(): lax.all_to_all(spread, TILE, split_axis=0, concat_axis=0, tiled=True)]
    all_to_all x1, waiting for transfers between devices: 17.1 us -> 27.2 us  [body(): lax.all_to_all(outgoing, TILE, split_axis=1, concat_axis=1, tiled=True)]
    all_gather x1, waiting for transfers between devices: 8.79 us -> 0.01 us  [body(): active_all = lax.all_gather(active, CHAN, axis=1, tiled=True)]
  transfers between devices with their start and end apart: 7 -> 6, of which waited for: 7 -> 4; matrix products, arithmetic and copies ran while one was open for 23% -> 19% of each run, Pallas kernels for 0% -> 0%
where the time goes in v2:
time: 158 us; the launch traced here: 157 us
  waiting for transfers between devices  75.7 us (48%)
  starting transfers between devices  29.2 us (18%)
  between operations  15.1 us (10%)
  other arithmetic  13.7 us (9%)
  matrix products  12.8 us (8%)
  local copies, waits for them, and re-layouts  10.5 us (7%)
    all_to_all x1, waiting for transfers between devices, body(): lax.all_to_all(outgoing, TILE, split_axis=1, concat_axis=1, tiled=True)  27.2 us
    all_to_all x1, waiting for transfers between devices, body(): lax.all_to_all(returning, TILE, split_axis=1, concat_axis=1, tiled=True)  21.6 us
    all_to_all x1, waiting for transfers between devices, tile_sum(): lax.all_to_all(spread, TILE, split_axis=0, concat_axis=0, tiled=True)  16.1 us
    all_to_all x1, starting transfers between devices, body(): lax.all_to_all(outgoing, TILE, split_axis=1, concat_axis=1, tiled=True)  12 us
    all_to_all x1, waiting for transfers between devices, tile_sum(): pieces = lax.all_to_all(rows, TILE, split_axis=0, concat_axis=0, tiled=True)  10.1 us
    all_to_all x1, starting transfers between devices, tile_sum(): lax.all_to_all(spread, TILE, split_axis=0, concat_axis=0, tiled=True)  6.06 us
    all_to_all x1, starting transfers between devices, body(): lax.all_to_all(returning, TILE, split_axis=1, concat_axis=1, tiled=True)  5.51 us
    all_to_all x1, starting transfers between devices, tile_sum(): pieces = lax.all_to_all(rows, TILE, split_axis=0, concat_axis=0, tiled=True)  5.5 us
  transfers between devices with their start and end apart: 6, of which 4 were waited for; matrix products, arithmetic and copies ran while one was open for 19% of the time, Pallas kernels for 0%

profile of v2, /device:TPU:8, one launch (start us, length us, event | category | flops | bytes accessed | tf_op | source)
XLA Modules:
  0.0 156.9 jit_solution(17260661308345343484)
XLA Ops:
  7.2 0.7 all-gather.6.cloned.1.call-update
  7.9 0.9 convert_bitcast_fusion
  8.9 0.6 reduce-window.6
  10.0 1.0 select_reduce_fusion
  11.8 1.7 %gather_fusion = bf16[384,8,128]{2,1,0:T(8,128)(2,1)S(1)} fusion(bf16[256,8,128]{2,1,0:T(8,128)(2,1)S(1)} %bitcast.140, s32[1024]{0:T(1024)S(1)} %pad_clamp_fusion.1), kind=kCustom, calls=%fused_computation | custom fusion | bytes 1574400 | tf_op jit(solution)/shard_map/jit(_take)/gather | solution.py:91
  13.5 3.1 %fusion.18 = bf16[1,384,8,128]{3,2,0,1:T(8,128)(2,1)} fusion(bf16[384,8,128]{2,1,0:T(8,128)(2,1)S(1)} %gather_fusion, pred[384]{0:T(512)(128)(4,1)S(1)} %compare_and_fusion, pred[384]{0:T(512)(128)(4,1)S(1)} %broadcast_in_dim.117), kind=kLoop, calls=%fused_computation.21 | loop fusion | flops 786432 | bytes 1573632 | tf_op jit(solution)/shard_map/jit(_where)/select_n | solution.py:92
  16.6 12.0 %all-to-all-start = ((bf16[1,384,8,128]{3,2,0,1:T(8,128)(2,1)}), bf16[1,384,8,128]{3,2,0,1:T(8,128)(2,1)S(1)}, u32[]{:S(2)}, u32[]{:S(2)}) async-start(bf16[1,384,8,128]{3,2,0,1:T(8,128)(2,1)} %fusion.18), calls=%async_computation | async-start | bytes 1572864 | tf_op jit(solution)/shard_map/all_to_all | solution.py:107
  29.2 0.7 constant_dynamic-slice_fusion
  29.9 0.6 iota_compare_fusion.8
  30.8 1.4 compare_select_fusion.1
  32.1 0.7 compare_and_fusion.1
  33.6 27.2 %all-to-all-done = bf16[1,384,8,128]{3,2,0,1:T(8,128)(2,1)S(1)} async-done(((bf16[1,384,8,128]{3,2,0,1:T(8,128)(2,1)}), bf16[1,384,8,128]{3,2,0,1:T(8,128)(2,1)S(1)}, u32[]{:S(2)}, u32[]{:S(2)}) %all-to-all-start) | async-done | bytes 786464 | tf_op jit(solution)/shard_map/all_to_all | solution.py:107
  60.8 0.8 gather_fusion.1
  61.7 3.9 %fusion.10 = bf16[1,1156,128]{2,1,0:T(8,128)(2,1)S(1)} fusion(bf16[1,1156,2048]{2,1,0:T(8,128)(2,1)} %param.10, bf16[256,8,128]{2,1,0:T(8,128)(2,1)S(1)} %gather_fusion.1, pred[256]{0:T(512)(128)(4,1)S(1)} %compare_and_fusion.1, pred[256]{0:T(512)(128)(4,1)S(1)} %iota_compare_fusion.8), kind=kOutput, calls=%fused_computation.8 | convolution fusion | flops 606749184 | bytes 5555712 | tf_op jit(solution)/shard_map/pk,bkc->bpc/dot_general | solution.py:111
  65.7 1.9 %convolution_bitcast_fusion = f32[1024,128]{0,1:T(8,128)S(1)} fusion(bf16[1,1024,512]{2,1,0:T(8,128)(2,1)} %all-gather.6.cloned.1.call-done, bf16[512,512]{1,0:T(8,128)(2,1)} %param.16, s32[]{:T(128)S(6)} %select_n.219), kind=kOutput, calls=%fused_computation.11 | convolution fusion | flops 134217728 | bytes 1703940 | tf_op jit(solution)/shard_map/dot_general | solution.py:125
  67.8 0.9 fusion.27
  69.4 0.7 select_maximum_fusion
  70.2 5.5 %all-to-all-start.2 = ((f32[64,1,1152]{2,1,0:T(1,128)}), f32[64,1,1152]{2,1,0:T(1,128)S(1)}, u32[]{:S(2)}, u32[]{:S(2)}) async-start(f32[64,1,1152]{2,1,0:T(1,128)} %bitcast.57), calls=%async_computation.2 | async-start | bytes 589824 | tf_op jit(solution)/shard_map/all_to_all | solution.py:56
  75.7 1.4 compare_select_fusion.3
  77.1 0.6 broadcast_multiply_fusion.8
  77.7 0.7 add_convert_fusion
  78.5 10.1 %all-to-all-done.2 = f32[64,1,1152]{2,1,0:T(1,128)S(1)} async-done(((f32[64,1,1152]{2,1,0:T(1,128)}), f32[64,1,1152]{2,1,0:T(1,128)S(1)}, u32[]{:S(2)}, u32[]{:S(2)}) %all-to-all-start.2) | async-done | bytes 294944 | tf_op jit(solution)/shard_map/all_to_all | solution.py:56
  88.8 0.9 broadcast_in_dim.129
  89.7 6.1 %all-to-all-start.3 = ((f32[64,1,1152]{2,1,0:T(1,128)}), f32[64,1,1152]{2,1,0:T(1,128)S(1)}, u32[]{:S(2)}, u32[]{:S(2)}) async-start(f32[64,1,1152]{2,1,0:T(1,128)} %broadcast_in_dim.129), calls=%async_computation.3 | async-start | bytes 589824 | tf_op jit(solution)/shard_map/all_to_all | solution.py:59
  95.7 3.3 %fusion.4 = bf16[1,2048,128]{1,2,0:T(8,128)(2,1)S(1)} fusion(bf16[1156,128]{1,0:T(8,128)(2,1)S(1)} %reshape.368, bf16[1,1156,2048]{2,1,0:T(8,128)(2,1)} %param.10), kind=kOutput, calls=%fused_computation.6 | convolution fusion | flops 606076928 | bytes 5555200 | tf_op jit(solution)/shard_map/pk,bpc->bkc/dot_general | solution.py:137
  100.1 1.4 copy.90
  101.5 16.1 %all-to-all-done.3 = f32[64,1,1152]{2,1,0:T(1,128)S(1)} async-done(((f32[64,1,1152]{2,1,0:T(1,128)}), f32[64,1,1152]{2,1,0:T(1,128)S(1)}, u32[]{:S(2)}, u32[]{:S(2)}) %all-to-all-start.3) | async-done | bytes 294944 | tf_op jit(solution)/shard_map/all_to_all | solution.py:59
  117.6 5.5 %all-to-all-start.1 = ((bf16[1,384,8,128]{3,2,0,1:T(8,128)(2,1)}), bf16[1,384,8,128]{3,2,0,1:T(8,128)(2,1)S(1)}, u32[]{:S(2)}, u32[]{:S(2)}) async-start(bf16[1,384,8,128]{3,2,0,1:T(8,128)(2,1)} %copy.90), calls=%async_computation.1 | async-start | bytes 1572864 | tf_op jit(solution)/shard_map/all_to_all | solution.py:147
  123.8 0.7 mul.295
  124.5 21.6 %all-to-all-done.1 = bf16[1,384,8,128]{3,2,0,1:T(8,128)(2,1)S(1)} async-done(((bf16[1,384,8,128]{3,2,0,1:T(8,128)(2,1)}), bf16[1,384,8,128]{3,2,0,1:T(8,128)(2,1)S(1)}, u32[]{:S(2)}, u32[]{:S(2)}) %all-to-all-start.1) | async-done | bytes 786464 | tf_op jit(solution)/shard_map/all_to_all | solution.py:147
  146.6 1.1 copy.99
  147.7 2.4 %fusion.13 = bf16[1,1024,128]{2,1,0:T(8,128)(2,1)} fusion(bf16[1024,512]{1,0:T(8,128)(2,1)} %all-gather.4.cloned.1.call-done, bf16[512,512]{1,0:T(8,128)(2,1)} %param.16, s32[]{:T(128)S(6)} %select_n.219), kind=kOutput, calls=%fused_computation.13 | convolution fusion | flops 134348800 | bytes 1441796 | tf_op jit(solution)/shard_map/dot_general | solution.py:121
  (63 shorter events, 5.6 us)
Async XLA Ops:
  7.2 4.6 %copy-start = (bf16[1,256,8,128]{3,2,1,0:T(8,128)(2,1)S(1)}, bf16[1,256,8,128]{3,2,1,0:T(8,128)(2,1)}, u32[]{:S(2)}) copy-start(bf16[1,256,8,128]{3,2,1,0:T(8,128)(2,1)} %param.9) | copy-start | bytes 1572868
  7.2 21.5 %copy-start.4 = (s32[64]{0:T(128)S(1)}, s32[64]{0:T(128)}, u32[]{:S(2)}) copy-start(s32[64]{0:T(128)} %param.13) | copy-start | bytes 772
  7.2 25.6 %copy-start.3 = (bf16[3,3,128]{2,1,0:T(4,128)(2,1)S(1)}, bf16[3,3,128]{2,1,0:T(4,128)(2,1)}, u32[]{:S(2)}) copy-start(bf16[3,3,128]{2,1,0:T(4,128)(2,1)} %param.15) | copy-start | bytes 6916
  7.2 58.5 %all-gather.6.cloned.1.call-start = ((), (), s32[]{:S(2)}) async-start(), calls=%async_computation.5 | async-start | bytes 1310720 | tf_op jit(solution)/shard_map/all_gather | solution.py:124
  16.6 44.2 %all-to-all-start = ((bf16[1,384,8,128]{3,2,0,1:T(8,128)(2,1)}), bf16[1,384,8,128]{3,2,0,1:T(8,128)(2,1)S(1)}, u32[]{:S(2)}, u32[]{:S(2)}) async-start(bf16[1,384,8,128]{3,2,0,1:T(8,128)(2,1)} %fusion.18), calls=%async_computation | async-start | bytes 1572864 | tf_op jit(solution)/shard_map/all_to_all | solution.py:107
  65.7 3.3 %copy-start.1 = (bf16[1,1024,512]{2,1,0:T(8,128)(2,1)S(1)}, bf16[1,1024,512]{2,1,0:T(8,128)(2,1)}, u32[]{:S(2)}) copy-start(bf16[1,1024,512]{2,1,0:T(8,128)(2,1)} %all-gather.6.cloned.1.call-done) | copy-start | bytes 3145732
  69.0 8.1 %copy-start.2 = (bf16[1,32,32,128]{3,2,1,0:T(8,128)(2,1)}, bf16[1,32,32,128]{3,2,1,0:T(8,128)(2,1)S(1)}, u32[]{:S(2)}) copy-start(bf16[1,32,32,128]{3,2,1,0:T(8,128)(2,1)S(1)} %multiply_convert_fusion) | copy-start | bytes 786436
  70.2 18.4 %all-to-all-start.2 = ((f32[64,1,1152]{2,1,0:T(1,128)}), f32[64,1,1152]{2,1,0:T(1,128)S(1)}, u32[]{:S(2)}, u32[]{:S(2)}) async-start(f32[64,1,1152]{2,1,0:T(1,128)} %bitcast.57), calls=%async_computation.2 | async-start | bytes 589824 | tf_op jit(solution)/shard_map/all_to_all | solution.py:56
  75.7 72.0 %all-gather.4.cloned.1.call-start = ((), (), s32[]{:S(2)}) async-start(), calls=%async_computation.4 | async-start | bytes 1310720 | tf_op jit(solution)/shard_map/all_gather | solution.py:120
  89.7 27.9 %all-to-all-start.3 = ((f32[64,1,1152]{2,1,0:T(1,128)}), f32[64,1,1152]{2,1,0:T(1,128)S(1)}, u32[]{:S(2)}, u32[]{:S(2)}) async-start(f32[64,1,1152]{2,1,0:T(1,128)} %broadcast_in_dim.129), calls=%async_computation.3 | async-start | bytes 589824 | tf_op jit(solution)/shard_map/all_to_all | solution.py:59
  117.6 28.5 %all-to-all-start.1 = ((bf16[1,384,8,128]{3,2,0,1:T(8,128)(2,1)}), bf16[1,384,8,128]{3,2,0,1:T(8,128)(2,1)S(1)}, u32[]{:S(2)}, u32[]{:S(2)}) async-start(bf16[1,384,8,128]{3,2,0,1:T(8,128)(2,1)} %copy.90), calls=%async_computation.1 | async-start | bytes 1572864 | tf_op jit(solution)/shard_map/all_to_all | solution.py:147
Sparse Core Ops, SparseCore 0:
  9.8 35.8 all-gather.5
  78.9 36.8 all-gather.3

commit v3 on v2

--- a/solution.py
+++ b/solution.py
@@ -49,15 +49,23 @@
     return (jnp.stack(tap_rows), grad_field)
 
 
-def tile_sum(flat, parts):
+def tile_partial(flat, parts):
     total = flat.shape[0]
     width = -(-total // (parts * 128)) * 128
     rows = jnp.pad(flat, (0, parts * width - total)).reshape(parts, width)
     pieces = lax.all_to_all(rows, TILE, split_axis=0, concat_axis=0, tiled=True)
-    mine = jnp.sum(pieces, axis=0)
-    spread = jnp.broadcast_to(mine[None, :], (parts, width))
-    whole = lax.all_to_all(spread, TILE, split_axis=0, concat_axis=0, tiled=True)
-    return whole.reshape(-1)[:total]
+    return jnp.sum(pieces, axis=0)
+
+
+def as_word_pair(value):
+    high = lax.reduce_precision(value, exponent_bits=8, mantissa_bits=7)
+    low = value - high
+    return jnp.concatenate([high.astype(jnp.bfloat16), low.astype(jnp.bfloat16)])
+
+
+def from_word_pair(words):
+    width = words.shape[-1] // 2
+    return words[..., :width].astype(jnp.float32) + words[..., width:].astype(jnp.float32)
 
 
 def body(
@@ -144,7 +152,21 @@
         preferred_element_type=jnp.float32,
     ).astype(jnp.bfloat16).reshape(batch_rows, tile_total * capacity, seg_len, chan_local)
     landing = jnp.where(slot_filled, slot_block, block_total)
-    arrived = lax.all_to_all(returning, TILE, split_axis=1, concat_axis=1, tiled=True)
+    grad_kernel = turn_kernel(grad_turned, turn, -1)
+    packed = jnp.concatenate([grad_kernel.reshape(-1), grad_mix.reshape(-1)])
+    my_slot = tile_partial(packed, tile_total)
+    slot_words = as_word_pair(my_slot)
+    block_width = capacity * seg_len * chan_local
+    payload = jnp.concatenate(
+        [
+            returning.reshape(tile_total, block_width),
+            jnp.broadcast_to(slot_words[None, :], (tile_total, slot_words.shape[0])),
+        ],
+        axis=1,
+    )
+    arrived_all = lax.all_to_all(payload, TILE, split_axis=0, concat_axis=0, tiled=True)
+    arrived = arrived_all[:, :block_width].reshape(batch_rows, tile_total * capacity, seg_len, chan_local)
+    packed = from_word_pair(arrived_all[:, block_width:]).reshape(-1)[: packed.shape[0]]
     block_ids = jnp.arange(block_total, dtype=jnp.int32)
     gather_back = (block_ids[:, None] == landing[None, :]).astype(jnp.bfloat16)
     summed = jnp.einsum(
@@ -152,9 +174,6 @@
         preferred_element_type=jnp.float32,
     )
     grad_latlon = summed.astype(jnp.bfloat16).reshape(batch_rows, block_total, seg_len, chan_local)
-    grad_kernel = turn_kernel(grad_turned, turn, -1)
-    packed = jnp.concatenate([grad_kernel.reshape(-1), grad_mix.reshape(-1)])
-    packed = tile_sum(packed, tile_total)
     kernel_sum = packed[: grad_kernel.size].reshape(grad_kernel.shape)
     mix_sum = packed[grad_kernel.size :].reshape(grad_mix.shape)
     factor = 1.0 / math.sqrt(batch_rows * tile_cells * tile_total)

time: 158 us -> 156 us (0.987)
  local copies, waits for them, and re-layouts: 10.5 us -> 18.3 us
  waiting for transfers between devices: 75.7 us -> 69.8 us
  starting transfers between devices: 29.2 us -> 23.9 us
  other arithmetic: 13.7 us -> 15.3 us
    all_to_all x3 -> x2, waiting for transfers between devices: 47.7 us -> 11.9 us  [the longest x1 6.14 us: tile_partial(): pieces = lax.all_to_all(rows, TILE, split_axis=0, concat_axis=0, tiled=True)]
    all_gather x1, waiting for transfers between devices: 0.01 us -> 30.6 us  [body(): active_all = lax.all_gather(active, CHAN, axis=1, tiled=True)]
    unnamed x12 -> x15, local copies, waits for them, and re-layouts: 1.17 us -> 8.97 us
    all_to_all x3 -> x2, starting transfers between devices: 17.1 us -> 11.8 us  [the longest x1 6.3 us: body(): lax.all_to_all(payload, TILE, split_axis=0, concat_axis=0, tiled=True)]
    all_to_all x0 -> x2, other arithmetic: none -> 1.62 us  [body(): lax.all_to_all(payload, TILE, split_axis=0, concat_axis=0, tiled=True)]
  transfers between devices with their start and end apart: 6 -> 5, of which waited for: 4 -> 4; matrix products, arithmetic and copies ran while one was open for 19% -> 18% of each run, Pallas kernels for 0% -> 0%
where the time goes in v3:
time: 156 us; the launch traced here: 155 us
  waiting for transfers between devices  69.8 us (45%)
  starting transfers between devices  23.9 us (15%)
  local copies, waits for them, and re-layouts  18.3 us (12%)
  other arithmetic  15.3 us (10%)
  between operations  15.2 us (10%)
  matrix products  12.7 us (8%)
    all_gather x1, waiting for transfers between devices, body(): active_all = lax.all_gather(active, CHAN, axis=1, tiled=True)  30.6 us
    all_to_all x1, waiting for transfers between devices, body(): lax.all_to_all(outgoing, TILE, split_axis=1, concat_axis=1, tiled=True)  25.9 us
    all_to_all x1, starting transfers between devices, body(): lax.all_to_all(outgoing, TILE, split_axis=1, concat_axis=1, tiled=True)  12 us
    unnamed x15, local copies, waits for them, and re-layouts  8.97 us
    all_to_all x1, starting transfers between devices, body(): lax.all_to_all(payload, TILE, split_axis=0, concat_axis=0, tiled=True)  6.3 us
    all_to_all x1, waiting for transfers between devices, tile_partial(): pieces = lax.all_to_all(rows, TILE, split_axis=0, concat_axis=0, tiled=True)  6.14 us
    all_to_all x1, waiting for transfers between devices, body(): lax.all_to_all(payload, TILE, split_axis=0, concat_axis=0, tiled=True)  5.79 us
    all_to_all x1, starting transfers between devices, tile_partial(): pieces = lax.all_to_all(rows, TILE, split_axis=0, concat_axis=0, tiled=True)  5.51 us
  transfers between devices with their start and end apart: 5, of which 4 were waited for; matrix products, arithmetic and copies ran while one was open for 18% of the time, Pallas kernels for 0%

profile of v3, /device:TPU:8, one launch (start us, length us, event | category | flops | bytes accessed | tf_op | source)
XLA Modules:
  0.0 155.2 jit_solution(7278160592824222360)
XLA Ops:
  7.2 0.7 all-gather.6.cloned.1.call-update
  7.9 0.9 convert_bitcast_fusion
  10.0 1.0 select_reduce_fusion
  11.8 1.7 %gather_fusion = bf16[384,8,128]{2,1,0:T(8,128)(2,1)S(1)} fusion(bf16[256,8,128]{2,1,0:T(8,128)(2,1)S(1)} %bitcast.138, s32[1024]{0:T(1024)S(1)} %pad_clamp_fusion.1), kind=kCustom, calls=%fused_computation | custom fusion | bytes 1574400 | tf_op jit(solution)/shard_map/jit(_take)/gather | solution.py:99
  13.5 3.1 %fusion.17 = bf16[1,384,8,128]{3,2,0,1:T(8,128)(2,1)} fusion(bf16[384,8,128]{2,1,0:T(8,128)(2,1)S(1)} %gather_fusion, pred[384]{0:T(512)(128)(4,1)S(1)} %compare_and_fusion, pred[384]{0:T(512)(128)(4,1)S(1)} %broadcast_in_dim.117), kind=kLoop, calls=%fused_computation.22 | loop fusion | flops 786432 | bytes 1573632 | tf_op jit(solution)/shard_map/jit(_where)/select_n | solution.py:100
  16.6 12.0 %all-to-all-start = ((bf16[1,384,8,128]{3,2,0,1:T(8,128)(2,1)}), bf16[1,384,8,128]{3,2,0,1:T(8,128)(2,1)S(1)}, u32[]{:S(2)}, u32[]{:S(2)}) async-start(bf16[1,384,8,128]{3,2,0,1:T(8,128)(2,1)} %fusion.17), calls=%async_computation | async-start | bytes 1572864 | tf_op jit(solution)/shard_map/all_to_all | solution.py:115
  29.2 0.7 constant_dynamic-slice_fusion
  30.8 1.4 compare_select_fusion.3
  32.1 1.4 compare_select_fusion.1
  34.2 0.7 compare_and_fusion.1
  35.0 25.9 %all-to-all-done = bf16[1,384,8,128]{3,2,0,1:T(8,128)(2,1)S(1)} async-done(((bf16[1,384,8,128]{3,2,0,1:T(8,128)(2,1)}), bf16[1,384,8,128]{3,2,0,1:T(8,128)(2,1)S(1)}, u32[]{:S(2)}, u32[]{:S(2)}) %all-to-all-start) | async-done | bytes 786464 | tf_op jit(solution)/shard_map/all_to_all | solution.py:115
  60.8 0.8 gather_fusion.1
  61.6 3.9 %fusion.10 = bf16[1,1156,128]{2,1,0:T(8,128)(2,1)S(1)} fusion(bf16[1,1156,2048]{2,1,0:T(8,128)(2,1)} %param.10, bf16[256,8,128]{2,1,0:T(8,128)(2,1)S(1)} %gather_fusion.1, pred[256]{0:T(512)(128)(4,1)S(1)} %compare_and_fusion.1, pred[256]{0:T(512)(128)(4,1)S(1)} %iota_compare_fusion.8), kind=kOutput, calls=%fused_computation.8 | convolution fusion | flops 606749184 | bytes 5555712 | tf_op jit(solution)/shard_map/pk,bkc->bpc/dot_general | solution.py:119
  65.7 1.8 %convolution_bitcast_fusion = f32[1024,128]{0,1:T(8,128)S(1)} fusion(bf16[1,1024,512]{2,1,0:T(8,128)(2,1)} %all-gather.6.cloned.1.call-done, bf16[512,512]{1,0:T(8,128)(2,1)} %param.16, s32[]{:T(128)S(6)} %select_n.219), kind=kOutput, calls=%fused_computation.12 | convolution fusion | flops 134217728 | bytes 1703940 | tf_op jit(solution)/shard_map/dot_general | solution.py:133
  67.7 0.9 fusion.26
  69.3 0.7 select_maximum_fusion
  70.1 5.5 %all-to-all-start.1 = ((f32[64,1,1152]{2,1,0:T(1,128)}), f32[64,1,1152]{2,1,0:T(1,128)S(1)}, u32[]{:S(2)}, u32[]{:S(2)}) async-start(f32[64,1,1152]{2,1,0:T(1,128)} %bitcast.53), calls=%async_computation.1 | async-start | bytes 589824 | tf_op jit(solution)/shard_map/all_to_all | solution.py:56
  76.1 0.8 add_convert_fusion
  77.0 3.3 %fusion.4 = bf16[1,2048,128]{1,2,0:T(8,128)(2,1)S(1)} fusion(bf16[1156,128]{1,0:T(8,128)(2,1)S(1)} %reshape.360, bf16[1,1156,2048]{2,1,0:T(8,128)(2,1)} %param.10), kind=kOutput, calls=%fused_computation.6 | convolution fusion | flops 606076928 | bytes 5555200 | tf_op jit(solution)/shard_map/pk,bpc->bkc/dot_general | solution.py:145
  81.6 0.7 reshape_reshape.4
  82.4 6.1 %all-to-all-done.1 = f32[64,1,1152]{2,1,0:T(1,128)S(1)} async-done(((f32[64,1,1152]{2,1,0:T(1,128)}), f32[64,1,1152]{2,1,0:T(1,128)S(1)}, u32[]{:S(2)}, u32[]{:S(2)}) %all-to-all-start.1) | async-done | bytes 294944 | tf_op jit(solution)/shard_map/all_to_all | solution.py:56
  89.4 1.5 reduce.7
  90.9 1.2 reshape.393
  92.1 6.3 %all-to-all-start.2 = ((bf16[64,2,4224]{2,1,0:T(2,128)(2,1)}), bf16[64,2,4224]{2,1,0:T(2,128)(2,1)}, u32[]{:S(2)}, u32[]{:S(2)}) async-start(bf16[64,2,4224]{2,1,0:T(2,128)(2,1)} %reshape.393), calls=%async_computation.2 | async-start | bytes 2162688 | tf_op jit(solution)/shard_map/all_to_all | solution.py:167
  98.4 0.7 all-gather.4.cloned.1.call-update
  99.2 30.6 %all-gather.4.cloned.1.call-done = bf16[1024,512]{1,0:T(8,128)(2,1)} async-done(((bf16[1024,128]{1,0:T(8,128)(2,1)}), bf16[1024,512]{1,0:T(8,128)(2,1)}) %all-gather.4.cloned.1.call-update) | async-done | bytes 1048592 | tf_op jit(solution)/shard_map/all_gather | solution.py:128
  129.8 2.4 %fusion.14 = bf16[1,1024,128]{2,1,0:T(8,128)(2,1)} fusion(bf16[1024,512]{1,0:T(8,128)(2,1)} %all-gather.4.cloned.1.call-done, bf16[512,512]{1,0:T(8,128)(2,1)} %param.16, s32[]{:T(128)S(6)} %select_n.219), kind=kOutput, calls=%fused_computation.14 | convolution fusion | flops 134348800 | bytes 1441796 | tf_op jit(solution)/shard_map/dot_general | solution.py:129
  132.1 5.8 %all-to-all-done.2 = bf16[64,2,4224]{2,1,0:T(2,128)(2,1)} async-done(((bf16[64,2,4224]{2,1,0:T(2,128)(2,1)}), bf16[64,2,4224]{2,1,0:T(2,128)(2,1)}, u32[]{:S(2)}, u32[]{:S(2)}) %all-to-all-start.2) | async-done | bytes 1081376 | tf_op jit(solution)/shard_map/all_to_all | solution.py:167
  137.9 6.5 %reshape.394 = bf16[64,1,8448]{2,1,0:T(2,128)(2,1)S(1)} reshape(bf16[64,2,4224]{2,1,0:T(2,128)(2,1)} %all-to-all-done.2) | data formatting | bytes 2162688
  144.7 0.7 reshape.364
  145.9 1.1 copy.121
  147.6 0.7 mul.295
  (73 shorter events, 8.6 us)
Async XLA Ops:
  7.2 4.6 %copy-start = (bf16[1,256,8,128]{3,2,1,0:T(8,128)(2,1)S(1)}, bf16[1,256,8,128]{3,2,1,0:T(8,128)(2,1)}, u32[]{:S(2)}) copy-start(bf16[1,256,8,128]{3,2,1,0:T(8,128)(2,1)} %param.9) | copy-start | bytes 1572868
  7.2 58.5 %all-gather.6.cloned.1.call-start = ((), (), s32[]{:S(2)}) async-start(), calls=%async_computation.4 | async-start | bytes 1310720 | tf_op jit(solution)/shard_map/all_gather | solution.py:132
  11.7 16.9 %copy-start.4 = (s32[64]{0:T(128)S(1)}, s32[64]{0:T(128)}, u32[]{:S(2)}) copy-start(s32[64]{0:T(128)} %param.13) | copy-start | bytes 772
  11.8 21.8 %copy-start.3 = (bf16[3,3,128]{2,1,0:T(4,128)(2,1)S(1)}, bf16[3,3,128]{2,1,0:T(4,128)(2,1)}, u32[]{:S(2)}) copy-start(bf16[3,3,128]{2,1,0:T(4,128)(2,1)} %param.15) | copy-start | bytes 6916
  16.6 44.2 %all-to-all-start = ((bf16[1,384,8,128]{3,2,0,1:T(8,128)(2,1)}), bf16[1,384,8,128]{3,2,0,1:T(8,128)(2,1)S(1)}, u32[]{:S(2)}, u32[]{:S(2)}) async-start(bf16[1,384,8,128]{3,2,0,1:T(8,128)(2,1)} %fusion.17), calls=%async_computation | async-start | bytes 1572864 | tf_op jit(solution)/shard_map/all_to_all | solution.py:115
  67.7 1.3 copy-start.1
  68.9 7.2 %copy-start.2 = (bf16[1,32,32,128]{3,2,1,0:T(8,128)(2,1)}, bf16[1,32,32,128]{3,2,1,0:T(8,128)(2,1)S(1)}, u32[]{:S(2)}) copy-start(bf16[1,32,32,128]{3,2,1,0:T(8,128)(2,1)S(1)} %multiply_convert_fusion) | copy-start | bytes 786436
  70.1 18.4 %all-to-all-start.1 = ((f32[64,1,1152]{2,1,0:T(1,128)}), f32[64,1,1152]{2,1,0:T(1,128)S(1)}, u32[]{:S(2)}, u32[]{:S(2)}) async-start(f32[64,1,1152]{2,1,0:T(1,128)} %bitcast.53), calls=%async_computation.1 | async-start | bytes 589824 | tf_op jit(solution)/shard_map/all_to_all | solution.py:56
  92.1 45.8 %all-to-all-start.2 = ((bf16[64,2,4224]{2,1,0:T(2,128)(2,1)}), bf16[64,2,4224]{2,1,0:T(2,128)(2,1)}, u32[]{:S(2)}, u32[]{:S(2)}) async-start(bf16[64,2,4224]{2,1,0:T(2,128)(2,1)} %reshape.393), calls=%async_computation.2 | async-start | bytes 2162688 | tf_op jit(solution)/shard_map/all_to_all | solution.py:167
  98.4 31.4 %all-gather.4.cloned.1.call-start = ((), (), s32[]{:S(2)}) async-start(), calls=%async_computation.3 | async-start | bytes 1310720 | tf_op jit(solution)/shard_map/all_gather | solution.py:128
Sparse Core Ops, SparseCore 0:
  9.8 35.8 all-gather.5
  101.6 28.1 all-gather.3
